TPU v7x, 128 devices: a whole 4x4x4 slice. The times are simulated.
128 devices in a mesh: req: 16 (over y, x), head: 8 (over z, core).
Axes of the slice: x: 4, y: 4, z: 4, core: 2. Of those that a mesh axis runs over, the one named last changes fastest.
Arguments:
- hidden_in: bfloat16 [4864, 3072], P('req', 'head'), may hold values from -6 to 6
- dec_query: bfloat16 [768, 3072], P('req', 'head'), may hold values from -5.5 to 5.5
- dec_key: bfloat16 [768, 3072], P('req', 'head'), may hold values from -6 to 6
- dec_value: bfloat16 [768, 3072], P('req', 'head'), may hold values from -6 to 6
- pre_query: bfloat16 [4096, 3072], P('req', 'head'), may hold values from -5.5 to 5.5
- pre_key: bfloat16 [4096, 3072], P('req', 'head'), may hold values from -6 to 6
- pre_value: bfloat16 [4096, 3072], P('req', 'head'), may hold values from -6 to 6
- cache_key: bfloat16 [32, 2048, 3072], P('req', None, 'head'), may hold values from -5.5 to 5.5
- cache_value: bfloat16 [32, 2048, 3072], P('req', None, 'head'), may hold values from -6 to 6
- group_of: int32 [768, 1], replicated, may hold values from 0 to 31; in each aligned block of 768 rows (0 to 767, 768 to 1535, ...) at most 48 rows name the same one
- cache_length: int32 [32], P('req'), may hold values from 256 to 2048, as said below
- stretch_start: int32 [16], P('req'), may hold values from 256 to 2048, as said below
- row_owner: int32 [4864, 1], P('req'), may hold values from 0 to 15; in each aligned block of 304 rows (0 to 303, 304 to 607, ...) at most 40 rows name the same one
- out_weight: bfloat16 [3072, 3072], P('head'), may hold values from -0.109375 to 0.109375
- norm_gain: float32 [3072], replicated, may hold values from 0.1 to 1.9
- gate_weight: bfloat16 [3072, 4096], P(None, 'head'), may hold values from -0.109375 to 0.109375
- up_weight: bfloat16 [3072, 4096], P(None, 'head'), may hold values from -0.109375 to 0.109375
- down_weight: bfloat16 [4096, 3072], P('head'), may hold values from -0.09375 to 0.09375
Outputs:
- layer_out: bfloat16 [10240, 3072], P(('req', 'head'))
Inputs may be any that keep to these rules, and one draw needn't show every extreme that they name: `group_of`: at most 48 requests share a cache group, exactly 48 in some group; every group has a request. `cache_length`: some group has all 2048 rows valid. `stretch_start`: some stretch follows all 2048 cached rows. `row_owner`: among the 304 rows of one index of req at most 40 share an owner, exactly 40 on some index.
All inputs are finite; a program needn't handle non-finite values.
Results may differ from a plain program's by a relative error of at most 0.02.
Values may be sent and summed in bfloat16 or wider, within the bound.
No kernel may reach another device: no remote copies, remote signals or barrier semaphores. Data moves between devices by JAX's collectives and lax.ppermute only.
A program may use at most 128 MiB of HBM per device.

v0:
```python
import math
import jax
import jax.numpy as jnp
from jax import lax
from jax.sharding import PartitionSpec as P

HD = 96
CAP = 48
eps_norm = 1e-05


def head_split(matrix):
    return matrix.reshape(matrix.shape[0], matrix.shape[1] // HD, HD)


def softmax_rows(scores, allowed):
    masked = jnp.where(allowed, scores, -jnp.inf)
    highest = jnp.max(masked, axis=-1, keepdims=True)
    raised = jnp.exp(masked - highest)
    return (raised / jnp.sum(raised, axis=-1, keepdims=True)).astype(jnp.bfloat16)


def on_device(
    hidden_in,
    dec_query,
    dec_key,
    dec_value,
    pre_query,
    pre_key,
    pre_value,
    cache_key,
    cache_value,
    group_of,
    cache_length,
    stretch_start,
    row_owner,
    out_weight,
    norm_gain,
    gate_weight,
    up_weight,
    down_weight,
):
    factor = 1.0 / math.sqrt(HD)
    width_here = dec_query.shape[1]
    queries_all, keys_own, values_own = (
        lax.all_gather(dec_query, "req", axis=0, tiled=True),
        lax.all_gather(dec_key, "req", axis=0, tiled=True),
        lax.all_gather(dec_value, "req", axis=0, tiled=True),
    )
    groups_here = cache_key.shape[0]
    length_cache = cache_key.shape[1]
    first_group = lax.axis_index("req") * groups_here
    members = group_of[:, 0]
    wanted = first_group + jnp.arange(groups_here, dtype=jnp.int32)
    belongs = (members[None, :] == wanted[:, None]).astype(jnp.int32)
    ranking = jnp.cumsum(belongs, axis=1) - 1
    places = jnp.arange(CAP, dtype=jnp.int32)
    chosen = (belongs[:, None, :] == 1) & (ranking[:, None, :] == places[None, :, None])
    chooser = chosen.reshape(groups_here * CAP, members.shape[0])
    stacked_in = jnp.concatenate([queries_all, keys_own, values_own], axis=1)
    picked = jnp.dot(
        chooser.astype(jnp.bfloat16), stacked_in, preferred_element_type=jnp.float32
    ).astype(jnp.bfloat16)
    positions = jnp.arange(length_cache)
    results = []
    for group_pos in range(groups_here):
        rows_block = picked[group_pos * CAP : (group_pos + 1) * CAP]
        picked_q = head_split(rows_block[:, :width_here])
        picked_k = head_split(rows_block[:, width_here : 2 * width_here])
        picked_v = head_split(rows_block[:, 2 * width_here :])
        cache_scores = (
            jnp.einsum(
                "qhd,khd->hqk",
                picked_q,
                head_split(cache_key[group_pos]),
                preferred_element_type=jnp.float32,
            )
            * factor
        )
        own_scores = (
            jnp.sum(picked_q.astype(jnp.float32) * picked_k.astype(jnp.float32), axis=-1).T * factor
        )
        scores = jnp.concatenate([cache_scores, own_scores[:, :, None]], axis=-1)
        allowed = jnp.concatenate([positions < cache_length[group_pos], jnp.ones((1,), bool)])[
            None, None, :
        ]
        weights = softmax_rows(scores, allowed)
        blended = jnp.einsum(
            "hqk,khd->qhd",
            weights[:, :, :length_cache],
            head_split(cache_value[group_pos]),
            preferred_element_type=jnp.float32,
        )
        blended = blended + weights[:, :, length_cache].astype(jnp.float32).T[
            :, :, None
        ] * picked_v.astype(jnp.float32)
        results.append(blended.reshape(CAP, width_here))
    stacked = jnp.concatenate(results, axis=0)
    spread_back = jnp.dot(chooser.astype(jnp.float32).T, stacked, precision=lax.Precision.HIGHEST)
    dec_out = lax.psum_scatter(
        spread_back.astype(jnp.bfloat16), "req", scatter_dimension=0, tiled=True
    )
    stretch_len = pre_query.shape[0]
    key_rows = jnp.concatenate([cache_key[0], pre_key], axis=0)
    value_rows = jnp.concatenate([cache_value[0], pre_value], axis=0)
    columns = jnp.arange(length_cache + stretch_len)
    row_numbers = jnp.arange(stretch_len)
    allowed_pre = jnp.where(
        columns[None, :] < length_cache,
        columns[None, :] < stretch_start[0],
        columns[None, :] - length_cache <= row_numbers[:, None],
    )
    pre_scores = (
        jnp.einsum(
            "qhd,khd->hqk",
            head_split(pre_query),
            head_split(key_rows),
            preferred_element_type=jnp.float32,
        )
        * factor
    )
    pre_weights = softmax_rows(pre_scores, allowed_pre[None])
    pre_mixed = jnp.einsum(
        "hqk,khd->qhd", pre_weights, head_split(value_rows), preferred_element_type=jnp.float32
    )
    pre_out = pre_mixed.reshape(stretch_len, width_here).astype(jnp.bfloat16)
    attn_rows = jnp.concatenate([dec_out, pre_out], axis=0)
    projected = jnp.dot(attn_rows, out_weight, preferred_element_type=jnp.float32)
    col_start = lax.axis_index("head") * width_here
    own_cols = lax.dynamic_slice_in_dim(projected, col_start, width_here, 1) + hidden_in.astype(
        jnp.float32
    )
    contribution = lax.dynamic_update_slice_in_dim(projected, own_cols, col_start, 1)
    req_count = lax.axis_size("req")
    row_count = contribution.shape[0]
    slot_rows = 8 * ((2 * row_count + 8 * req_count - 1) // (8 * req_count))
    owners = row_owner[:, 0]
    onehot_owner = (owners[:, None] == jnp.arange(req_count, dtype=jnp.int32)[None, :]).astype(
        jnp.int32
    )
    before = jnp.sum((jnp.cumsum(onehot_owner, axis=0) - 1) * onehot_owner, axis=1)
    target = owners * slot_rows + before
    placing = (
        target[None, :] == jnp.arange(req_count * slot_rows, dtype=jnp.int32)[:, None]
    ).astype(jnp.bfloat16)
    residual = lax.psum(contribution.astype(jnp.bfloat16), "head")
    outgoing = jnp.dot(placing, residual, preferred_element_type=jnp.float32).astype(jnp.bfloat16)
    arrived = lax.all_to_all(outgoing, "req", split_axis=0, concat_axis=0, tiled=True)
    arrived_wide = arrived.astype(jnp.float32)
    squares = jnp.mean(jnp.square(arrived_wide), axis=-1, keepdims=True)
    normed = (arrived_wide * lax.rsqrt(squares + eps_norm) * norm_gain).astype(jnp.bfloat16)
    gate_act = jnp.dot(normed, gate_weight, preferred_element_type=jnp.float32)
    up_act = jnp.dot(normed, up_weight, preferred_element_type=jnp.float32)
    hidden = (jax.nn.silu(gate_act) * up_act).astype(jnp.bfloat16)
    rows_here = arrived.shape[0] // lax.axis_size("head")
    down_sum = lax.psum_scatter(
        jnp.dot(hidden, down_weight, preferred_element_type=jnp.float32).astype(jnp.bfloat16),
        "head",
        scatter_dimension=0,
        tiled=True,
    ).astype(jnp.float32)
    own_rows = lax.dynamic_slice_in_dim(
        arrived_wide, lax.axis_index("head") * rows_here, rows_here, 0
    )
    return (own_rows + down_sum).astype(jnp.bfloat16)


def solution(mesh):
    placed = (
        P("req", "head"),
        P("req", "head"),
        P("req", "head"),
        P("req", "head"),
        P("req", "head"),
        P("req", "head"),
        P("req", "head"),
        P("req", None, "head"),
        P("req", None, "head"),
        P(),
        P("req"),
        P("req"),
        P("req", None),
        P("head", None),
        P(),
        P(None, "head"),
        P(None, "head"),
        P("head", None),
    )
    return jax.shard_map(
        on_device, mesh=mesh, in_specs=placed, out_specs=P(("req", "head"), None), check_vma=False
    )
```

profile of v0, /device:TPU:0, one launch (start us, length us, event | category | flops | bytes accessed | tf_op | source)
XLA Modules:
  0.0 390.3 jit_solution(7005297331430344854)
XLA Ops:
  6.6 1.5 fusion.83
  8.1 0.7 iota_compare_fusion.8
  8.8 1.3 iota_compare_fusion.7
  10.0 0.7 reduce.3
  10.9 0.6 reduce-window.16
  11.4 0.2 slice_reduce_fusion.1
  11.7 0.2 reduce-window.19
  11.9 24.6 %all_gather.9 = bf16[768,384]{1,0:T(8,128)(2,1)S(1)} all-gather(bf16[48,384]{1,0:T(8,128)(2,1)} %param.19), channel_id=1, replica_groups=mesh['req'=16,'head'=8] {'req'}, dimensions={0}, use_global_device_ids=true | all-gather | bytes 626688 | tf_op jit(solution)/shard_map/all_gather | solution.py:46
  36.5 23.5 %all_gather.10 = bf16[768,384]{1,0:T(8,128)(2,1)S(1)} all-gather(bf16[48,384]{1,0:T(8,128)(2,1)} %param.20), channel_id=1, replica_groups=mesh['req'=16,'head'=8] {'req'}, dimensions={0}, use_global_device_ids=true | all-gather | bytes 626688 | tf_op jit(solution)/shard_map/all_gather | solution.py:47
  60.0 21.9 %all_gather.11 = bf16[768,384]{1,0:T(8,128)(2,1)S(1)} all-gather(bf16[48,384]{1,0:T(8,128)(2,1)} %param.21), channel_id=1, replica_groups=mesh['req'=16,'head'=8] {'req'}, dimensions={0}, use_global_device_ids=true | all-gather | bytes 626688 | tf_op jit(solution)/shard_map/all_gather | solution.py:48
  82.1 0.4 convolution_convert_fusion.2
  82.5 0.2 copy-done.6
  82.7 0.7 slice_convert_fusion.2
  83.5 0.9 reshape.228
  84.6 1.0 reshape.234
  85.6 0.1 multiply_reduce_fusion.1
  85.7 1.1 copy.80
  86.8 1.0 reshape.232
  87.9 0.6 multiply_bitcast_fusion.1
  88.5 1.1 copy.73
  89.7 3.9 fusion.81
  93.5 2.6 copy.77
  96.2 1.8 convolution_multiply_fusion
  98.0 0.5 fusion.87
  98.5 0.2 divide_convert_fusion.2
  98.7 0.9 copy-done.3
  99.7 2.6 copy.70
  102.3 1.8 convolution_multiply_fusion.1
  104.1 0.5 fusion.88
  104.5 0.2 divide_convert_fusion.3
  104.7 0.9 copy-done.4
  105.7 0.5 copy-done.5
  106.2 1.9 fusion.82
  108.2 2.6 copy.81
  110.8 2.3 fusion.31
  113.3 2.7 copy.74
  115.9 2.3 fusion.32
  118.5 1.5 convolution_convert_fusion.3
  120.0 0.2 all-reduce.4.cloned.1.call-start
  120.9 0.6 iota_compare_fusion.5
  121.5 1.1 copy.86
  122.6 1.1 copy.85
  123.6 1.7 copy.84
  125.4 3.8 fusion.12
  129.2 4.9 %fusion.84 = f32[4,256]{1,0:T(4,128)S(1)} fusion(pred[256,2304]{0,1:T(8,128)(4,1)} %fusion.12, bf16[256,4,96]{0,2,1:T(8,128)(2,1)S(1)} %bitcast.97, bf16[256,4,96]{0,2,1:T(8,128)(2,1)S(1)} %bitcast.99, bf16[2048,4,96]{0,2,1:T(8,128)(2,1)} %bitcast.90), kind=kOutput, calls=%fused_computation.125 | convolution fusion | flops 465963264 | bytes 2560000 | tf_op jit(solution)/shard_map/sub | solution.py:19
  134.0 7.6 %fusion.28 = bf16[4,96,256]{2,1,0:T(8,128)(2,1)} fusion(f32[4,256]{1,0:T(4,128)S(1)} %fusion.84, bf16[256,4,96]{0,2,1:T(8,128)(2,1)} %bitcast.101, bf16[2048,4,96]{0,2,1:T(8,128)(2,1)} %bitcast.93, pred[256,2304]{0,1:T(8,128)(4,1)} %fusion.12, bf16[256,4,96]{0,2,1:T(8,128)(2,1)S(1)} %bitcast.98, bf16[256,4,96]{0,2,1:T(8,128)(2,1)S(1)} %bitcast.100, ...), kind=kOutput, calls=%fused_computation.45 | convolution fusion | flops 924945664 | bytes 4526080 | tf_op jit(solution)/shard_map/hqk,khd->qhd/dot_general | solution.py:123
  141.7 51.4 %reduce-scatter.7.cloned.1.call-done = bf16[48,384]{1,0:T(8,128)(2,1)} async-done(((bf16[768,384]{1,0:T(8,128)(2,1)}), bf16[48,384]{1,0:T(8,128)(2,1)}) %reduce-scatter.7.cloned.1.call-update) | async-done | bytes 36880
  193.0 0.9 copy.88
  193.9 3.1 fusion.44
  197.1 1.5 convert_element_type.133
  198.6 0.3 reduce-scatter.5.cloned.1.call-start
  198.9 0.9 reduce-window.14
  199.8 0.2 slice_reduce_fusion
  200.2 63.4 %all-reduce.4.cloned.1.call-done = bf16[304,3072]{1,0:T(8,128)(2,1)} async-done(((bf16[304,3072]{1,0:T(8,128)(2,1)}), bf16[304,3072]{1,0:T(8,128)(2,1)}) %all-reduce.4.cloned.1.call-update) | async-done | bytes 1867792 | tf_op jit(solution)/shard_map/psum | solution.py:146
  263.6 3.7 convolution_convert_fusion.1
  267.3 52.8 %all_to_all.9 = bf16[16,40,3072]{2,1,0:T(8,128)(2,1)S(1)} all-to-all(bf16[16,40,3072]{2,1,0:T(8,128)(2,1)S(1)} %bitcast.96), channel_id=1, replica_groups=mesh['req'=16,'head'=8] {'req'}, dimensions={0} | all-to-all | bytes 7864320 | tf_op jit(solution)/shard_map/all_to_all | solution.py:148
  320.1 0.8 multiply_reduce_fusion
  320.9 1.1 copy-done.1
  322.2 6.9 %multiply_convert_fusion = (bf16[640,3072]{1,0:T(8,128)(2,1)S(1)}, f32[16,40,3072]{2,1,0:T(8,128)}) fusion(f32[3072]{0:T(1024)S(1)} %copy-done.10, f32[640]{0:T(1024)S(1)} %rsqrt.12, bf16[16,40,3072]{2,1,0:T(8,128)(2,1)} %copy-done.1), kind=kLoop, calls=%fused_computation.7 | loop fusion | flops 7864320 | bytes 15743488 | tf_op jit(solution)/shard_map/convert_element_type | solution.py:151
  329.1 2.0 copy-done.2
  331.1 3.2 fusion.89
  334.4 9.7 %convolution_convert_fusion = bf16[640,3072]{1,0:T(8,128)(2,1)} fusion(bf16[512,3072]{1,0:T(8,128)(2,1)S(1)} %copy-done, bf16[640,3072]{1,0:T(8,128)(2,1)} %copy-done.2, bf16[3072,512]{1,0:T(8,128)(2,1)} %param.34, f32[640,512]{1,0:T(8,128)} %fusion.89), kind=kOutput, calls=%fused_computation.9 | convolution fusion | flops 4030464000 | bytes 15466496 | tf_op jit(solution)/shard_map/dot_general | solution.py:157
  344.1 37.5 %reduce-scatter.5.cloned.1.call-done = bf16[80,3072]{1,0:T(8,128)(2,1)} async-done(((bf16[640,3072]{1,0:T(8,128)(2,1)}), bf16[80,3072]{1,0:T(8,128)(2,1)}) %reduce-scatter.5.cloned.1.call-update) | async-done | bytes 491536 | tf_op jit(solution)/shard_map/reduce_scatter | solution.py:156
  381.6 2.2 add_convert_fusion
  (57 shorter events, 1.8 us)
Async XLA Ops:
  6.5 327.8 %copy-start = (bf16[512,3072]{1,0:T(8,128)(2,1)S(1)}, bf16[512,3072]{1,0:T(8,128)(2,1)}, u32[]{:S(2)}) copy-start(bf16[512,3072]{1,0:T(8,128)(2,1)} %param.35) | copy-start | bytes 9437188
  6.5 186.5 %reduce-scatter.7.cloned.1.call-start = ((), (), s32[]{:S(2)}) async-start(), calls=%async_computation.5 | async-start | bytes 626688
  82.1 0.6 copy-start.6
  96.2 1.8 copy-start.11
  96.2 1.8 copy-start.9
  98.7 0.9 copy-start.3
  104.0 2.2 copy-start.5
  104.7 0.9 copy-start.4
  115.9 2.5 copy-start.7
  115.9 4.9 %copy-start.12 = (s32[304,1]{0,1:T(1,128)S(1)}, s32[304,1]{0,1:T(1,128)}, u32[]{:S(2)}) copy-start(s32[304,1]{0,1:T(1,128)} %param.30) | copy-start | bytes 3652
  120.0 143.6 %all-reduce.4.cloned.1.call-start = ((), (), s32[]{:S(2)}) async-start(), calls=%async_computation.3 | async-start | bytes 3735552 | tf_op jit(solution)/shard_map/psum | solution.py:146
  193.9 3.1 copy-start.8
  198.6 182.9 %reduce-scatter.5.cloned.1.call-start = ((), (), s32[]{:S(2)}) async-start(), calls=%async_computation.4 | async-start | bytes 4423680 | tf_op jit(solution)/shard_map/reduce_scatter | solution.py:156
  320.1 2.0 copy-start.1
  320.1 2.1 copy-start.10
  322.2 8.9 %copy-start.13 = (bf16[3072,512]{1,0:T(8,128)(2,1)S(1)}, bf16[3072,512]{1,0:T(8,128)(2,1)}, u32[]{:S(2)}) copy-start(bf16[3072,512]{1,0:T(8,128)(2,1)} %param.33) | copy-start | bytes 9437188
  329.1 2.0 copy-start.2
Sparse Core Ops, SparseCore 0:
  120.1 72.9 reduce-scatter.6
  198.8 64.7 all-reduce.3
  344.2 37.3 reduce-scatter.4
where the time goes:
time: 392 us; the launch traced here: 390 us
  waiting for transfers between devices  152 us (39%)
  blocking collectives  123 us (31%)
  matrix products  42.3 us (11%)
  local copies, waits for them, and re-layouts  34.5 us (9%)
  other arithmetic  23.7 us (6%)
  between operations  14.1 us (4%)
    psum x1, waiting for transfers between devices, on_device(): residual = lax.psum(contribution.astype(jnp.bfloat16), 'head')  63.4 us
    all_to_all x1, blocking collectives, on_device(): lax.all_to_all(outgoing, 'req', split_axis=0, concat_axis=0, tiled=True)  52.8 us
    unnamed x4, waiting for transfers between devices  51.4 us
    reduce_scatter x1, waiting for transfers between devices, on_device(): lax.psum_scatter(jnp.dot(hidden, down_weight, preferred_element_type=jnp....  37.5 us
    all_gather x1, blocking collectives, on_device(): lax.all_gather(dec_query, 'req', axis=0, tiled=True)  24.6 us
    all_gather x1, blocking collectives, on_device(): lax.all_gather(dec_key, 'req', axis=0, tiled=True)  23.5 us
    all_gather x1, blocking collectives, on_device(): lax.all_gather(dec_value, 'req', axis=0, tiled=True)  21.9 us
    dot_general x1, matrix products, on_device(): jnp.dot(hidden, down_weight, preferred_element_type=jnp.float32)  9.69 us
  transfers between devices with their start and end apart: 3, of which 3 were waited for; matrix products, arithmetic and copies ran while one was open for 6% of the time, Pallas kernels for 0%

commit v1 on v0

--- a/solution.py
+++ b/solution.py
@@ -143,7 +143,7 @@
     placing = (
         target[None, :] == jnp.arange(req_count * slot_rows, dtype=jnp.int32)[:, None]
     ).astype(jnp.bfloat16)
-    residual = lax.psum(contribution.astype(jnp.bfloat16), "head")
+    residual = jnp.sum(lax.all_gather(contribution.astype(jnp.bfloat16), "head"), axis=0)
     outgoing = jnp.dot(placing, residual, preferred_element_type=jnp.float32).astype(jnp.bfloat16)
     arrived = lax.all_to_all(outgoing, "req", split_axis=0, concat_axis=0, tiled=True)
     arrived_wide = arrived.astype(jnp.float32)

time: 392 us -> 413 us (1.054)
  other arithmetic: 23.7 us -> 33.8 us
  waiting for transfers between devices: 152 us -> 161 us
    all_gather x0 -> x1, waiting for transfers between devices: none -> 75 us  [on_device(): lax.all_gather(contribution.astype(jnp.bfloat16), 'head')]
    psum x1 -> x0, waiting for transfers between devices: 63.4 us -> none  [on_device(): residual = lax.psum(contribution.astype(jnp.bfloat16), 'head')]
    reduce_sum x0 -> x1, other arithmetic: none -> 9.89 us  [on_device(): jnp.sum(lax.all_gather(contribution.astype(jnp.bfloat16), 'head'), axis=0)]
  transfers between devices with their start and end apart: 3 -> 3, of which waited for: 3 -> 3; matrix products, arithmetic and copies ran while one was open for 6% -> 5% of each run, Pallas kernels for 0% -> 0%
where the time goes in v1:
time: 413 us; the launch traced here: 412 us
  waiting for transfers between devices  161 us (39%)
  blocking collectives  125 us (30%)
  matrix products  42.3 us (10%)
  local copies, waits for them, and re-layouts  34.9 us (8%)
  other arithmetic  33.8 us (8%)
  between operations  14.1 us (3%)
    all_gather x1, waiting for transfers between devices, on_device(): lax.all_gather(contribution.astype(jnp.bfloat16), 'head')  75 us
    all_to_all x1, blocking collectives, on_device(): lax.all_to_all(outgoing, 'req', split_axis=0, concat_axis=0, tiled=True)  55.1 us
    unnamed x4, waiting for transfers between devices  51.3 us
    reduce_scatter x1, waiting for transfers between devices, on_device(): lax.psum_scatter(jnp.dot(hidden, down_weight, preferred_element_type=jnp....  34.5 us
    all_gather x1, blocking collectives, on_device(): lax.all_gather(dec_query, 'req', axis=0, tiled=True)  24.6 us
    all_gather x1, blocking collectives, on_device(): lax.all_gather(dec_key, 'req', axis=0, tiled=True)  23.5 us
    all_gather x1, blocking collectives, on_device(): lax.all_gather(dec_value, 'req', axis=0, tiled=True)  21.9 us
    unnamed x32, local copies, waits for them, and re-layouts  9.93 us
  transfers between devices with their start and end apart: 3, of which 3 were waited for; matrix products, arithmetic and copies ran while one was open for 5% of the time, Pallas kernels for 0%

profile of v1, /device:TPU:0, one launch (start us, length us, event | category | flops | bytes accessed | tf_op | source)
XLA Modules:
  0.0 411.5 jit_solution(17405445527574301663)
XLA Ops:
  6.6 1.5 fusion.83
  8.1 0.7 iota_compare_fusion.8
  8.8 1.3 iota_compare_fusion.7
  10.0 0.7 reduce.4
  10.9 0.6 reduce-window.16
  11.4 0.2 slice_reduce_fusion.1
  11.7 0.2 reduce-window.19
  11.9 24.6 %all_gather.15 = bf16[768,384]{1,0:T(8,128)(2,1)S(1)} all-gather(bf16[48,384]{1,0:T(8,128)(2,1)} %param.19), channel_id=1, replica_groups=mesh['req'=16,'head'=8] {'req'}, dimensions={0}, use_global_device_ids=true | all-gather | bytes 626688 | tf_op jit(solution)/shard_map/all_gather | solution.py:46
  36.5 23.5 %all_gather.16 = bf16[768,384]{1,0:T(8,128)(2,1)S(1)} all-gather(bf16[48,384]{1,0:T(8,128)(2,1)} %param.20), channel_id=1, replica_groups=mesh['req'=16,'head'=8] {'req'}, dimensions={0}, use_global_device_ids=true | all-gather | bytes 626688 | tf_op jit(solution)/shard_map/all_gather | solution.py:47
  60.0 21.9 %all_gather.17 = bf16[768,384]{1,0:T(8,128)(2,1)S(1)} all-gather(bf16[48,384]{1,0:T(8,128)(2,1)} %param.21), channel_id=1, replica_groups=mesh['req'=16,'head'=8] {'req'}, dimensions={0}, use_global_device_ids=true | all-gather | bytes 626688 | tf_op jit(solution)/shard_map/all_gather | solution.py:48
  82.1 0.4 convolution_convert_fusion.2
  82.5 0.2 copy-done.6
  82.7 0.7 slice_convert_fusion.2
  83.5 0.9 reshape.228
  84.6 1.0 reshape.234
  85.7 1.1 copy.80
  86.8 1.0 reshape.232
  87.9 0.6 multiply_bitcast_fusion.1
  88.5 1.1 copy.73
  89.7 3.9 fusion.81
  93.5 2.6 copy.77
  96.2 1.8 convolution_multiply_fusion
  98.0 0.5 fusion.87
  98.5 0.2 divide_convert_fusion.2
  98.7 0.9 copy-done.3
  99.7 2.6 copy.70
  102.3 1.8 convolution_multiply_fusion.1
  104.1 0.5 fusion.88
  104.7 0.9 copy-done.4
  105.7 0.5 copy-done.5
  106.2 1.9 fusion.82
  108.2 2.6 copy.81
  110.8 2.3 fusion.31
  113.3 2.7 copy.74
  115.9 2.3 fusion.32
  118.4 1.5 convolution_convert_fusion.3
  120.0 0.2 all-gather.3.cloned.1.call-start
  120.8 0.6 iota_compare_fusion.5
  121.4 1.1 copy.86
  122.5 1.1 copy.85
  123.6 1.7 copy.84
  125.3 3.9 fusion.12
  129.3 4.9 %fusion.84 = f32[4,256]{1,0:T(4,128)S(1)} fusion(pred[256,2304]{0,1:T(8,128)(4,1)} %fusion.12, bf16[256,4,96]{0,2,1:T(8,128)(2,1)S(1)} %bitcast.99, bf16[256,4,96]{0,2,1:T(8,128)(2,1)S(1)} %bitcast.101, bf16[2048,4,96]{0,2,1:T(8,128)(2,1)} %bitcast.92), kind=kOutput, calls=%fused_computation.125 | convolution fusion | flops 465963264 | bytes 2560000 | tf_op jit(solution)/shard_map/sub | solution.py:19
  134.2 7.6 %fusion.28 = bf16[4,96,256]{2,1,0:T(8,128)(2,1)} fusion(f32[4,256]{1,0:T(4,128)S(1)} %fusion.84, bf16[256,4,96]{0,2,1:T(8,128)(2,1)} %bitcast.103, bf16[2048,4,96]{0,2,1:T(8,128)(2,1)} %bitcast.95, pred[256,2304]{0,1:T(8,128)(4,1)} %fusion.12, bf16[256,4,96]{0,2,1:T(8,128)(2,1)S(1)} %bitcast.100, bf16[256,4,96]{0,2,1:T(8,128)(2,1)S(1)} %bitcast.102, ...), kind=kOutput, calls=%fused_computation.45 | convolution fusion | flops 924945664 | bytes 4526080 | tf_op jit(solution)/shard_map/hqk,khd->qhd/dot_general | solution.py:123
  141.8 51.3 %reduce-scatter.7.cloned.1.call-done = bf16[48,384]{1,0:T(8,128)(2,1)} async-done(((bf16[768,384]{1,0:T(8,128)(2,1)}), bf16[48,384]{1,0:T(8,128)(2,1)}) %reduce-scatter.7.cloned.1.call-update) | async-done | bytes 36880
  193.0 0.9 copy.88
  193.9 3.1 fusion.44
  197.1 1.5 convert_element_type.135
  198.7 0.3 reduce-scatter.5.cloned.1.call-start
  198.9 0.4 copy-done.12
  199.4 0.9 reduce-window.14
  200.2 0.2 slice_reduce_fusion
  200.6 75.0 %all-gather.3.cloned.1.call-done = bf16[2432,3072]{1,0:T(8,128)(2,1)} async-done(((bf16[304,3072]{1,0:T(8,128)(2,1)}), bf16[2432,3072]{1,0:T(8,128)(2,1)}) %all-gather.3.cloned.1.call-update) | async-done | bytes 14942224 | tf_op jit(solution)/shard_map/all_gather | solution.py:146
  275.6 9.9 %reduce_sum.81 = bf16[304,3072]{1,0:T(8,128)(2,1)} reduce(bf16[8,304,3072]{2,1,0:T(8,128)(2,1)} %bitcast.89, bf16[]{:T(256)} %constant.57.clone.1), dimensions={0}, to_apply=%region_14.15 | reduce | flops 6537216 | bytes 16809986 | tf_op jit(solution)/shard_map/reduce_sum | solution.py:146
  285.5 3.7 convolution_convert_fusion.1
  289.2 55.1 %all_to_all.9 = bf16[16,40,3072]{2,1,0:T(8,128)(2,1)S(1)} all-to-all(bf16[16,40,3072]{2,1,0:T(8,128)(2,1)S(1)} %bitcast.98), channel_id=1, replica_groups=mesh['req'=16,'head'=8] {'req'}, dimensions={0} | all-to-all | bytes 7864320 | tf_op jit(solution)/shard_map/all_to_all | solution.py:148
  344.3 0.8 multiply_reduce_fusion
  345.2 1.1 copy-done.1
  346.4 6.9 %multiply_convert_fusion = (bf16[640,3072]{1,0:T(8,128)(2,1)S(1)}, f32[16,40,3072]{2,1,0:T(8,128)}) fusion(f32[3072]{0:T(1024)S(1)} %copy-done.10, f32[640]{0:T(1024)S(1)} %rsqrt.12, bf16[16,40,3072]{2,1,0:T(8,128)(2,1)} %copy-done.1), kind=kLoop, calls=%fused_computation.7 | loop fusion | flops 7864320 | bytes 15743488 | tf_op jit(solution)/shard_map/convert_element_type | solution.py:151
  353.4 2.0 copy-done.2
  355.3 3.2 fusion.89
  358.6 9.7 %convolution_convert_fusion = bf16[640,3072]{1,0:T(8,128)(2,1)} fusion(bf16[512,3072]{1,0:T(8,128)(2,1)S(1)} %copy-done, bf16[640,3072]{1,0:T(8,128)(2,1)} %copy-done.2, bf16[3072,512]{1,0:T(8,128)(2,1)} %param.34, f32[640,512]{1,0:T(8,128)} %fusion.89), kind=kOutput, calls=%fused_computation.9 | convolution fusion | flops 4030464000 | bytes 15466496 | tf_op jit(solution)/shard_map/dot_general | solution.py:157
  368.3 34.5 %reduce-scatter.5.cloned.1.call-done = bf16[80,3072]{1,0:T(8,128)(2,1)} async-done(((bf16[640,3072]{1,0:T(8,128)(2,1)}), bf16[80,3072]{1,0:T(8,128)(2,1)}) %reduce-scatter.5.cloned.1.call-update) | async-done | bytes 491536 | tf_op jit(solution)/shard_map/reduce_scatter | solution.py:156
  402.8 2.2 add_convert_fusion
  (58 shorter events, 2.1 us)
Async XLA Ops:
  6.5 352.0 %copy-start = (bf16[512,3072]{1,0:T(8,128)(2,1)S(1)}, bf16[512,3072]{1,0:T(8,128)(2,1)}, u32[]{:S(2)}) copy-start(bf16[512,3072]{1,0:T(8,128)(2,1)} %param.35) | copy-start | bytes 9437188
  6.5 186.5 %reduce-scatter.7.cloned.1.call-start = ((), (), s32[]{:S(2)}) async-start(), calls=%async_computation.5 | async-start | bytes 626688
  82.1 0.6 copy-start.6
  96.2 1.8 copy-start.11
  96.2 1.8 copy-start.9
  98.7 0.9 copy-start.3
  104.0 2.2 copy-start.5
  104.7 0.9 copy-start.4
  115.9 2.5 copy-start.7
  120.0 155.7 %all-gather.3.cloned.1.call-start = ((), (), s32[]{:S(2)}) async-start(), calls=%async_computation.4 | async-start | bytes 16809984 | tf_op jit(solution)/shard_map/all_gather | solution.py:146
  193.9 3.1 copy-start.8
  198.6 0.7 copy-start.12
  198.7 204.1 %reduce-scatter.5.cloned.1.call-start = ((), (), s32[]{:S(2)}) async-start(), calls=%async_computation.3 | async-start | bytes 4423680 | tf_op jit(solution)/shard_map/reduce_scatter | solution.py:156
  344.3 2.0 copy-start.1
  344.3 2.1 copy-start.10
  346.4 8.9 %copy-start.13 = (bf16[3072,512]{1,0:T(8,128)(2,1)S(1)}, bf16[3072,512]{1,0:T(8,128)(2,1)}, u32[]{:S(2)}) copy-start(bf16[3072,512]{1,0:T(8,128)(2,1)} %param.33) | copy-start | bytes 9437188
  353.4 2.0 copy-start.2
Sparse Core Ops, SparseCore 0:
  120.1 72.9 reduce-scatter.6
  198.8 76.8 all-gather.2
  368.4 34.2 reduce-scatter.4
